TPU v7x, 32 devices: a whole 2x2x4 slice. The times are simulated.
32 devices in a mesh: grid: 8 (over y, x, core), band: 4 (over z).
Axes of the slice: x: 2, y: 2, z: 4, core: 2. Of those that a mesh axis runs over, the one named last changes fastest.
Arguments:
- occupied: bfloat16 [1024, 32, 24, 128], P('band', 'grid'), may hold values from -6 to 6
- potential: float32 [32, 24, 128], P('grid'), may hold values from 0.2 to 4
- shifts: float32 [64], P('band'), may hold values from 0.5 to 4
- source_term: float32 [64, 32, 24, 128], P('band', 'grid'), may hold values from -125 to 125
Outputs:
- solution: float32 [64, 32, 24, 128], P('band', 'grid')
- residual: float32 [64, 32, 24, 128], P('band', 'grid')
All inputs are finite; a program needn't handle non-finite values.
Results may differ from a plain program's by a relative error of at most 0.022.
Values may be sent and summed in bfloat16 or wider, within the bound.
No kernel may reach another device: no remote copies, remote signals or barrier semaphores. Data moves between devices by JAX's collectives and lax.ppermute only.
A program may use at most 128 MiB of HBM per device.

v0:
```python
import math
import jax
import jax.numpy as jnp
from jax import lax
from jax.sharding import PartitionSpec as P

ITERS = 2
COEFFICIENTS = (-205.0 / 72.0, 8.0 / 5.0, -1.0 / 5.0, 8.0 / 315.0, -1.0 / 560.0)


def with_halo(shard, sides, width):
    for axis, dim in sides:
        peers, length = (lax.axis_size(axis), shard.shape[dim])
        up = [(i, (i + 1) % peers) for i in range(peers - 1)]
        down = [(j, i) for i, j in up]
        last = lax.slice_in_dim(shard, length - width, length, axis=dim)
        leading = lax.slice_in_dim(shard, 0, width, axis=dim)
        before = lax.ppermute(last, axis, up)
        after = lax.ppermute(leading, axis, down)
        shard = jnp.concatenate([before, shard, after], axis=dim)
    return shard


def second_sum(padded, extent_x, extent_y, extent_z):
    middle = padded[:, 4 : 4 + extent_x, 4 : 4 + extent_y, 4 : 4 + extent_z]
    summed = 3.0 * COEFFICIENTS[0] * middle
    for offset in range(1, 5):
        along_x = (
            padded[:, 4 + offset : 4 + offset + extent_x, 4 : 4 + extent_y, 4 : 4 + extent_z]
            + padded[:, 4 - offset : 4 - offset + extent_x, 4 : 4 + extent_y, 4 : 4 + extent_z]
        )
        along_y = (
            padded[:, 4 : 4 + extent_x, 4 + offset : 4 + offset + extent_y, 4 : 4 + extent_z]
            + padded[:, 4 : 4 + extent_x, 4 - offset : 4 - offset + extent_y, 4 : 4 + extent_z]
        )
        along_z = (
            padded[:, 4 : 4 + extent_x, 4 : 4 + extent_y, 4 + offset : 4 + offset + extent_z]
            + padded[:, 4 : 4 + extent_x, 4 : 4 + extent_y, 4 - offset : 4 - offset + extent_z]
        )
        summed = (
            summed
            + COEFFICIENTS[offset] * along_x
            + COEFFICIENTS[offset] * along_y
            + COEFFICIENTS[offset] * along_z
        )
    return summed


def inner_product(first_field, second_field):
    return jnp.sum(first_field * second_field, axis=(1, 2, 3))


def expand(vector):
    return vector[:, None, None, None]


def body(occupied, potential, shifts, source_term):
    local_bands, width_x, width_y, width_z = source_term.shape
    local_occupied = occupied.shape[0]
    band_count = lax.axis_size("band")
    local_cells = width_x * width_y * width_z
    weight_scale = 2.0 / math.sqrt(
        local_occupied * band_count * local_cells * lax.axis_size("grid")
    )
    occupied_rows = occupied.reshape(local_occupied, local_cells)
    potential_shift = potential[None] + shifts[:, None, None, None]
    solution = jnp.zeros_like(source_term)
    residual = source_term
    direction = source_term
    norm_now = lax.psum(inner_product(source_term, source_term), "grid")
    for iteration in range(ITERS):
        padded = with_halo(direction.astype(jnp.bfloat16), (("grid", 1),), 4).astype(
            direction.dtype
        )
        padded = jnp.pad(padded, ((0, 0), (0, 0), (4, 4), (4, 4)))
        kinetic = -0.5 * second_sum(padded, width_x, width_y, width_z)
        rounded = direction.astype(jnp.bfloat16).reshape(local_bands, local_cells)
        partial_margin = lax.dot_general(
            occupied_rows,
            lax.all_gather(rounded, "band", axis=0, tiled=True),
            (((1,), (1,)), ((), ())),
            preferred_element_type=jnp.float32,
        )
        margins = lax.psum(partial_margin, "grid")
        scaled = (margins * weight_scale).astype(jnp.bfloat16)
        projected = lax.psum_scatter(
            lax.dot_general(
                scaled, occupied_rows, (((0,), (0,)), ((), ())), preferred_element_type=jnp.float32
            ).astype(jnp.bfloat16),
            "band",
            scatter_dimension=0,
            tiled=True,
        ).astype(jnp.float32)
        applied = kinetic + potential_shift * direction + projected.reshape(direction.shape)
        curvature = lax.psum(inner_product(direction, applied), "grid")
        step_size = norm_now / curvature
        solution = solution + expand(step_size) * direction
        residual = residual - expand(step_size) * applied
        if iteration + 1 < ITERS:
            norm_next = lax.psum(inner_product(residual, residual), "grid")
            direction = residual + expand(norm_next / norm_now) * direction
            norm_now = norm_next
    return (solution, residual)


def solution(mesh):
    in_specs = (
        P("band", "grid", None, None),
        P("grid", None, None),
        P("band"),
        P("band", "grid", None, None),
    )
    out_specs = (P("band", "grid", None, None), P("band", "grid", None, None))
    return jax.shard_map(body, mesh=mesh, in_specs=in_specs, out_specs=out_specs, check_vma=False)
```

profile of v0, /device:TPU:0, one launch (start us, length us, event | category | flops | bytes accessed | tf_op | source)
XLA Modules:
  0.0 345.8 jit_solution(5779249794180429042)
XLA Ops:
  7.2 1.2 convert_element_type.31
  8.4 0.9 copy.32
  9.4 40.6 %all-gather.3.cloned.1.call-done = bf16[64,12288]{1,0:T(8,128)(2,1)} async-done(((bf16[16,12288]{1,0:T(8,128)(2,1)}), bf16[64,12288]{1,0:T(8,128)(2,1)}) %all-gather.3.cloned.1.call-update) | async-done | bytes 1572880 | tf_op jit(solution)/shard_map/all_gather | solution.py:80
  50.0 5.8 %fusion.4 = f32[256,64]{1,0:T(8,128)} fusion(bf16[64,12288]{1,0:T(8,128)(2,1)} %all-gather.3.cloned.1.call-done, bf16[32,8,96,128]{3,2,1,0:T(8,128)(2,1)} %bitcast.35), kind=kOutput, calls=%fused_computation.38 | convolution fusion | flops 402653184 | bytes 7929856 | tf_op jit(solution)/shard_map/dot_general | solution.py:78
  55.9 51.9 %all-reduce.6.cloned.1.call-done = f32[256,64]{1,0:T(8,128)} async-done(((f32[256,64]{1,0:T(8,128)}), f32[256,64]{1,0:T(8,128)}) %all-reduce.6.cloned.1.call-update) | async-done | bytes 65552 | tf_op jit(solution)/shard_map/psum | solution.py:84
  107.8 6.2 %convolution_convert_fusion.1 = bf16[64,12288]{1,0:T(8,128)(2,1)} fusion(bf16[32,8,96,128]{3,2,1,0:T(8,128)(2,1)} %bitcast.36, f32[256,64]{1,0:T(8,128)} %all-reduce.6.cloned.1.call-done), kind=kOutput, calls=%fused_computation.33 | convolution fusion | flops 403472384 | bytes 7929856 | tf_op jit(solution)/shard_map/dot_general | solution.py:87
  114.0 1.4 collective-permute-start.1
  115.5 3.1 collective-permute-start
  118.5 1.3 collective-permute-done
  119.8 0.2 maximum_convert_fusion
  120.0 28.8 %reduce-scatter.3.cloned.1.call-done = bf16[16,12288]{1,0:T(8,128)(2,1)} async-done(((bf16[64,12288]{1,0:T(8,128)(2,1)}), bf16[16,12288]{1,0:T(8,128)(2,1)}) %reduce-scatter.3.cloned.1.call-update) | async-done | bytes 393232 | tf_op jit(solution)/shard_map/reduce_scatter | solution.py:86
  148.8 1.0 convert_bitcast_fusion.1
  149.8 0.2 copy.8
  150.0 3.8 %multiply_reduce_fusion.2 = (f32[16]{0:T(128)S(1)}, f32[16]{0:T(128)S(1)}, f32[16,4,24,128]{3,2,1,0:T(8,128)}) fusion(f32[16,4,24,128]{3,2,1,0:T(8,128)S(1)} %copy-done, f32[16,4,24,128]{3,2,1,0:T(8,128)S(1)} %bitcast.41, f32[16]{0:T(128)S(1)} %copy-done.2, f32[4,24,128]{2,1,0:T(8,128)} %param.5, f32[16,12,24,128]{3,2,1,0:T(8,128)S(1)} %maximum_convert_fusion), kind=kLoop, calls=%fused_computation.135 | loop fusion | flops 9043936 | bytes 11846272 | tf_op jit(solution)/shard_map/reduce_sum | solution.py:50
  153.8 13.4 %all-reduce.2 = (f32[16]{0:T(128)S(1)}, f32[16]{0:T(128)S(1)}) all-reduce(f32[16]{0:T(128)S(1)} %get-tuple-element.3, f32[16]{0:T(128)S(1)} %get-tuple-element.2), channel_id=1, replica_groups=mesh['grid'=8,'band'=4] {'grid'}, use_global_device_ids=true, to_apply=%region_1.0 | all-reduce | flops 32 | bytes 256 | tf_op jit(solution)/shard_map/psum | solution.py:70
  167.3 1.4 multiply_reduce_fusion.1
  168.7 11.8 %psum.45 = f32[16]{0:T(128)S(1)} all-reduce(f32[16]{0:T(128)S(1)} %multiply_reduce_fusion.1), channel_id=1, replica_groups=mesh['grid'=8,'band'=4] {'grid'}, use_global_device_ids=true, to_apply=%region_7.8 | all-reduce | flops 16 | bytes 128 | tf_op jit(solution)/shard_map/psum | solution.py:100
  180.5 2.3 fusion.86
  182.8 0.9 copy.31
  183.7 34.6 %all-gather.5.cloned.1.call-done = bf16[64,12288]{1,0:T(8,128)(2,1)} async-done(((bf16[16,12288]{1,0:T(8,128)(2,1)}), bf16[64,12288]{1,0:T(8,128)(2,1)}) %all-gather.5.cloned.1.call-update) | async-done | bytes 1572880 | tf_op jit(solution)/shard_map/all_gather | solution.py:80
  218.3 5.9 %fusion.10 = f32[256,64]{1,0:T(8,128)} fusion(bf16[64,12288]{1,0:T(8,128)(2,1)} %all-gather.5.cloned.1.call-done, bf16[32,8,96,128]{3,2,1,0:T(8,128)(2,1)} %bitcast.37), kind=kOutput, calls=%fused_computation.46 | convolution fusion | flops 402653184 | bytes 7929856 | tf_op jit(solution)/shard_map/dot_general | solution.py:78
  224.3 51.9 %all-reduce.8.cloned.1.call-done = f32[256,64]{1,0:T(8,128)} async-done(((f32[256,64]{1,0:T(8,128)}), f32[256,64]{1,0:T(8,128)}) %all-reduce.8.cloned.1.call-update) | async-done | bytes 65552 | tf_op jit(solution)/shard_map/psum | solution.py:84
  276.2 6.2 %convolution_convert_fusion = bf16[64,12288]{1,0:T(8,128)(2,1)} fusion(bf16[32,8,96,128]{3,2,1,0:T(8,128)(2,1)} %bitcast.38, f32[256,64]{1,0:T(8,128)} %all-reduce.8.cloned.1.call-done), kind=kOutput, calls=%fused_computation.32 | convolution fusion | flops 403472384 | bytes 7929856 | tf_op jit(solution)/shard_map/dot_general | solution.py:87
  282.4 1.3 collective-permute-start.3
  283.7 3.1 collective-permute-start.2
  286.7 1.3 collective-permute-done.2
  288.0 0.2 maximum_convert_fusion.1
  288.2 29.0 %reduce-scatter.5.cloned.1.call-done = bf16[16,12288]{1,0:T(8,128)(2,1)} async-done(((bf16[64,12288]{1,0:T(8,128)(2,1)}), bf16[16,12288]{1,0:T(8,128)(2,1)}) %reduce-scatter.5.cloned.1.call-update) | async-done | bytes 393232 | tf_op jit(solution)/shard_map/reduce_scatter | solution.py:86
  317.2 1.1 convert_bitcast_fusion
  318.5 3.9 %multiply_reduce_fusion = (f32[16]{0:T(128)S(1)}, f32[16,4,24,128]{3,2,1,0:T(8,128)}) fusion(f32[16,4,24,128]{3,2,1,0:T(8,128)S(1)} %copy-done.1, f32[16,4,24,128]{3,2,1,0:T(8,128)S(1)} %bitcast.42, f32[16]{0:T(128)S(1)} %copy-done.2, f32[4,24,128]{2,1,0:T(8,128)} %param.5, f32[16,12,24,128]{3,2,1,0:T(8,128)S(1)} %maximum_convert_fusion.1), kind=kLoop, calls=%fused_computation.131 | loop fusion | flops 8650736 | bytes 11846208 | tf_op jit(solution)/shard_map/reduce_sum | solution.py:50
  322.3 13.4 %psum.47 = f32[16]{0:T(128)S(1)} all-reduce(f32[16]{0:T(128)S(1)} %get-tuple-element.6), channel_id=1, replica_groups=mesh['grid'=8,'band'=4] {'grid'}, use_global_device_ids=true, to_apply=%region_11.12 | all-reduce | flops 16 | bytes 128 | tf_op jit(solution)/shard_map/psum | solution.py:95
  335.8 3.2 multiply_subtract_fusion
  (24 shorter events, 0.5 us)
Async XLA Ops:
  7.2 42.8 %all-gather.3.cloned.1.call-start = ((), (), s32[]{:S(2)}) async-start(), calls=%async_computation.2 | async-start | bytes 1966080 | tf_op jit(solution)/shard_map/all_gather | solution.py:80
  9.3 98.4 %all-reduce.6.cloned.1.call-start = ((), (), s32[]{:S(2)}) async-start(), calls=%async_computation.3 | async-start | bytes 262144 | tf_op jit(solution)/shard_map/psum | solution.py:84
  55.8 92.9 %reduce-scatter.3.cloned.1.call-start = ((), (), s32[]{:S(2)}) async-start(), calls=%async_computation.4 | async-start | bytes 1966080 | tf_op jit(solution)/shard_map/reduce_scatter | solution.py:86
  113.9 36.0 %copy-start = (f32[16,4,24,128]{3,2,1,0:T(8,128)S(1)}, f32[16,4,24,128]{3,2,1,0:T(8,128)}, u32[]{:S(2)}) copy-start(f32[16,4,24,128]{3,2,1,0:T(8,128)} %param.7) | copy-start | bytes 2359300
  114.0 36.0 %copy-start.2 = (f32[16]{0:T(128)S(1)}, f32[16]{0:T(128)}, u32[]{:S(2)}) copy-start(f32[16]{0:T(128)} %param.6) | copy-start | bytes 196
  114.0 104.4 %all-gather.5.cloned.1.call-start = ((), (), s32[]{:S(2)}) async-start(), calls=%async_computation.5 | async-start | bytes 1966080 | tf_op jit(solution)/shard_map/all_gather | solution.py:80
  114.0 4.5 %collective-permute-start.1 = (bf16[16,4,24,128]{3,2,1,0:T(8,128)(2,1)S(1)}, bf16[16,4,24,128]{3,2,1,0:T(8,128)(2,1)S(1)}, u32[]{:S(2)}, u32[]{:S(2)}) collective-permute-start(bf16[16,4,24,128]{3,2,1,0:T(8,128)(2,1)S(1)} %convert_element_type.31), channel_id=1, source_target_pairs={{4,0},{8,4},{12,8},{16,12},{20,16},{24,20},{28,24},{5,1},{9,5},{13... | collective-permute-start | bytes 1179656 | tf_op jit(solution)/shard_map/ppermute | solution.py:19
  115.5 4.4 %collective-permute-start = (bf16[16,4,24,128]{3,2,1,0:T(8,128)(2,1)S(1)}, bf16[16,4,24,128]{3,2,1,0:T(8,128)(2,1)S(1)}, u32[]{:S(2)}, u32[]{:S(2)}) collective-permute-start(bf16[16,4,24,128]{3,2,1,0:T(8,128)(2,1)S(1)} %convert_element_type.31), channel_id=1, source_target_pairs={{0,4},{4,8},{8,12},{12,16},{16,20},{20,24},{24,28},{1,5},{5,9},{9,... | collective-permute-start | bytes 1179656 | tf_op jit(solution)/shard_map/ppermute | solution.py:18
  183.7 92.5 %all-reduce.8.cloned.1.call-start = ((), (), s32[]{:S(2)}) async-start(), calls=%async_computation.6 | async-start | bytes 262144 | tf_op jit(solution)/shard_map/psum | solution.py:84
  224.2 93.0 %reduce-scatter.5.cloned.1.call-start = ((), (), s32[]{:S(2)}) async-start(), calls=%async_computation.7 | async-start | bytes 1966080 | tf_op jit(solution)/shard_map/reduce_scatter | solution.py:86
  282.4 4.4 %collective-permute-start.3 = (bf16[16,4,24,128]{3,2,1,0:T(8,128)(2,1)S(1)}, bf16[16,4,24,128]{3,2,1,0:T(8,128)(2,1)S(1)}, u32[]{:S(2)}, u32[]{:S(2)}) collective-permute-start(bf16[16,4,24,128]{3,2,1,0:T(8,128)(2,1)S(1)} %get-tuple-element.8), channel_id=1, source_target_pairs={{4,0},{8,4},{12,8},{16,12},{20,16},{24,20},{28,24},{5,1},{9,5},{13... | collective-permute-start | bytes 1179656 | tf_op jit(solution)/shard_map/ppermute | solution.py:19
  283.7 4.4 %collective-permute-start.2 = (bf16[16,4,24,128]{3,2,1,0:T(8,128)(2,1)S(1)}, bf16[16,4,24,128]{3,2,1,0:T(8,128)(2,1)S(1)}, u32[]{:S(2)}, u32[]{:S(2)}) collective-permute-start(bf16[16,4,24,128]{3,2,1,0:T(8,128)(2,1)S(1)} %get-tuple-element.8), channel_id=1, source_target_pairs={{0,4},{4,8},{8,12},{12,16},{16,20},{20,24},{24,28},{1,5},{5,9},{9,... | collective-permute-start | bytes 1179656 | tf_op jit(solution)/shard_map/ppermute | solution.py:18
  317.2 1.3 copy-start.1
Sparse Core Ops, SparseCore 0:
  10.1 39.7 all-gather.2
  56.0 51.7 all-reduce.5
  114.1 34.6 reduce-scatter.2
  183.8 34.4 all-gather.4
  224.4 51.7 all-reduce.7
  282.5 34.6 reduce-scatter.4
where the time goes:
time: 346 us
  waiting for transfers between devices  239 us (69%)
  blocking collectives  38.6 us (11%)
  matrix products  24 us (7%)
  other arithmetic  18.3 us (5%)
  between operations  14.2 us (4%)
  starting transfers between devices  9.07 us (3%)
    psum x2, waiting for transfers between devices, body(): margins = lax.psum(partial_margin, 'grid')  104 us
    all_gather x2, waiting for transfers between devices, body(): lax.all_gather(rounded, 'band', axis=0, tiled=True)  75.2 us
    reduce_scatter x2, waiting for transfers between devices, body(): lax.psum_scatter(lax.dot_general(scaled, occupied_rows, (((0,), (0,)), ((...  57.8 us
    psum x1, blocking collectives, body(): curvature = lax.psum(inner_product(direction, applied), 'grid')  13.4 us
    psum x1, blocking collectives, body(): norm_now = lax.psum(inner_product(source_term, source_term), 'grid')  13.4 us
    dot_general x2, matrix products, body(): lax.dot_general(scaled, occupied_rows, (((0,), (0,)), ((), ())), preferre...  12.3 us
    psum x1, blocking collectives, body(): norm_next = lax.psum(inner_product(residual, residual), 'grid')  11.8 us
    dot_general x2, matrix products, body(): lax.dot_general(occupied_rows, lax.all_gather(rounded, 'band', axis=0, ti...  11.7 us
  transfers between devices with their start and end apart: 10, of which 8 were waited for; matrix products, arithmetic and copies ran while one was open for 0% of the time, Pallas kernels for 0%

commit v1 on v0

--- a/solution.py
+++ b/solution.py
@@ -1,3 +1,4 @@
+import functools
 import math
 import jax
 import jax.numpy as jnp
@@ -6,6 +7,45 @@
 
 ITERS = 2
 COEFFICIENTS = (-205.0 / 72.0, 8.0 / 5.0, -1.0 / 5.0, 8.0 / 315.0, -1.0 / 560.0)
+
+
+def arrange_knots_by_axis(page, shard_axis):
+    arr_now = jax.lax.axis_index(shard_axis)
+    answer = jax.lax.axis_size(shard_axis)
+    all_rows = []
+    w1, block_now, spare = (answer, arr_now, page.shape[0])
+    for dev_i, s in enumerate(page.shape):
+        all_rows.append(s * w1 if dev_i == 0 else s)
+    high = val = page
+    next_value = lax.dynamic_update_slice_in_dim(
+        jnp.zeros(all_rows, page.dtype), page, block_now * spare, axis=0
+    )
+    rr = 1
+    while rr < w1 // 2 + 1:
+        cards = []
+        dev_i = 0
+        while dev_i < w1:
+            cards.append((dev_i, (dev_i + 1) % w1))
+            dev_i = dev_i + 1
+        high = jax.lax.ppermute(high, axis_name=shard_axis, perm=cards)
+        next_value = lax.dynamic_update_slice_in_dim(
+            next_value, high, (block_now - rr) % w1 * spare, axis=0
+        )
+        if 2 * rr < w1:
+            rows = []
+            dev_i = 0
+            while dev_i < w1:
+                rows.append((dev_i, (dev_i - 1) % w1))
+                dev_i += 1
+            val = jax.lax.ppermute(val, axis_name=shard_axis, perm=rows)
+            next_value = lax.dynamic_update_slice_in_dim(
+                next_value, val, (block_now + rr) % w1 * spare, axis=0
+            )
+        rr += 1
+    return next_value
+
+
+note_vectors_on_mesh = functools.partial(arrange_knots_by_axis, shard_axis="band")
 
 
 def with_halo(shard, sides, width):
@@ -77,7 +117,7 @@
         rounded = direction.astype(jnp.bfloat16).reshape(local_bands, local_cells)
         partial_margin = lax.dot_general(
             occupied_rows,
-            lax.all_gather(rounded, "band", axis=0, tiled=True),
+            note_vectors_on_mesh(rounded),
             (((1,), (1,)), ((), ())),
             preferred_element_type=jnp.float32,
         )

time: 346 us -> 324 us (0.936)
  waiting for transfers between devices: 239 us -> 207 us
  starting transfers between devices: 9.07 us -> 22.8 us
    all_gather x2 -> x0, waiting for transfers between devices: 75.2 us -> none  [body(): lax.all_gather(rounded, 'band', axis=0, tiled=True)]
    ppermute x0 -> x6, waiting for transfers between devices: none -> 46.3 us  [the longest x4 38.2 us: arrange_knots_by_axis(): high = jax.lax.ppermute(high, axis_name=shard_axis, perm=cards)]
    ppermute x0 -> x6, starting transfers between devices: none -> 13.7 us  [the longest x4 7.84 us: arrange_knots_by_axis(): high = jax.lax.ppermute(high, axis_name=shard_axis, perm=cards)]
  transfers between devices with their start and end apart: 10 -> 14, of which waited for: 8 -> 12; matrix products, arithmetic and copies ran while one was open for 0% -> 0% of each run, Pallas kernels for 0% -> 0%
where the time goes in v1:
time: 324 us; the launch traced here: 323 us
  waiting for transfers between devices  207 us (64%)
  blocking collectives  38.8 us (12%)
  matrix products  23.5 us (7%)
  starting transfers between devices  22.8 us (7%)
  other arithmetic  15.6 us (5%)
  between operations  14 us (4%)
    psum x2, waiting for transfers between devices, body(): margins = lax.psum(partial_margin, 'grid')  101 us
    reduce_scatter x2, waiting for transfers between devices, body(): lax.psum_scatter(lax.dot_general(scaled, occupied_rows, (((0,), (0,)), ((...  57.9 us
    ppermute x4, waiting for transfers between devices, arrange_knots_by_axis(): high = jax.lax.ppermute(high, axis_name=shard_axis, perm=cards)  38.2 us
    psum x1, blocking collectives, body(): norm_now = lax.psum(inner_product(source_term, source_term), 'grid')  13.6 us
    psum x1, blocking collectives, body(): curvature = lax.psum(inner_product(direction, applied), 'grid')  13.4 us
    dot_general x2, matrix products, body(): lax.dot_general(scaled, occupied_rows, (((0,), (0,)), ((), ())), preferre...  12.3 us
    psum x1, blocking collectives, body(): norm_next = lax.psum(inner_product(residual, residual), 'grid')  11.8 us
    dot_general x2, matrix products, body(): lax.dot_general(occupied_rows, note_vectors_on_mesh(rounded), (((1,), (1,...  11.2 us
  transfers between devices with their start and end apart: 14, of which 12 were waited for; matrix products, arithmetic and copies ran while one was open for 0% of the time, Pallas kernels for 0%

profile of v1, /device:TPU:0, one launch (start us, length us, event | category | flops | bytes accessed | tf_op | source)
XLA Modules:
  0.0 323.5 jit_solution(13511933812761241231)
XLA Ops:
  7.2 1.2 convert_element_type.31
  8.6 3.1 collective-permute-start.2
  11.6 2.1 collective-permute-start.3
  14.0 9.6 %collective-permute-done.2 = bf16[16,12288]{1,0:T(8,128)(2,1)S(1)} collective-permute-done((bf16[16,12288]{1,0:T(8,128)(2,1)S(1)}, bf16[16,12288]{1,0:T(8,128)(2,1)S(1)}, u32[]{:S(2)}, u32[]{:S(2)}) %collective-permute-start.2) | collective-permute-done | bytes 393248 | tf_op jit(solution)/shard_map/ppermute | solution.py:30
  23.7 7.2 %collective-permute-done.3 = bf16[16,12288]{1,0:T(8,128)(2,1)S(1)} collective-permute-done((bf16[16,12288]{1,0:T(8,128)(2,1)S(1)}, bf16[16,12288]{1,0:T(8,128)(2,1)S(1)}, u32[]{:S(2)}, u32[]{:S(2)}) %collective-permute-start.3) | collective-permute-done | bytes 393248 | tf_op jit(solution)/shard_map/ppermute | solution.py:40
  30.9 8.8 %collective-permute-done.4 = bf16[16,12288]{1,0:T(8,128)(2,1)S(1)} collective-permute-done((bf16[16,12288]{1,0:T(8,128)(2,1)S(1)}, bf16[16,12288]{1,0:T(8,128)(2,1)S(1)}, u32[]{:S(2)}, u32[]{:S(2)}) %collective-permute-start.4) | collective-permute-done | bytes 393248 | tf_op jit(solution)/shard_map/ppermute | solution.py:30
  39.7 5.6 %fusion.10 = f32[256,64]{0,1:T(8,128)} fusion(bf16[64,12288]{1,0:T(8,128)(2,1)S(1)} %constant_dynamic-update-slice_fusion.4, bf16[32,8,96,128]{3,2,1,0:T(8,128)(2,1)} %bitcast.43), kind=kOutput, calls=%fused_computation.48 | convolution fusion | flops 402653184 | bytes 7929856 | tf_op jit(solution)/shard_map/dot_general | solution.py:118
  45.4 51.9 %all-reduce.6.cloned.1.call-done = f32[256,64]{0,1:T(8,128)} async-done(((f32[256,64]{0,1:T(8,128)}), f32[256,64]{0,1:T(8,128)}) %all-reduce.6.cloned.1.call-update) | async-done | bytes 65552 | tf_op jit(solution)/shard_map/psum | solution.py:124
  97.3 6.1 %convolution_convert_fusion.1 = bf16[64,12288]{1,0:T(8,128)(2,1)} fusion(bf16[32,8,96,128]{3,2,1,0:T(8,128)(2,1)} %bitcast.44, f32[256,64]{0,1:T(8,128)} %all-reduce.6.cloned.1.call-done), kind=kOutput, calls=%fused_computation.33 | convolution fusion | flops 403472384 | bytes 7929856 | tf_op jit(solution)/shard_map/dot_general | solution.py:127
  103.5 1.3 collective-permute-start.1
  104.8 3.1 collective-permute-start
  107.9 1.3 collective-permute-done
  109.4 28.9 %reduce-scatter.3.cloned.1.call-done = bf16[16,12288]{1,0:T(8,128)(2,1)} async-done(((bf16[64,12288]{1,0:T(8,128)(2,1)}), bf16[16,12288]{1,0:T(8,128)(2,1)}) %reduce-scatter.3.cloned.1.call-update) | async-done | bytes 393232 | tf_op jit(solution)/shard_map/reduce_scatter | solution.py:126
  139.5 3.0 multiply_reduce_fusion.2
  142.6 13.6 %all-reduce.2 = (f32[16]{0:T(128)S(1)}, f32[16]{0:T(128)S(1)}) all-reduce(f32[16]{0:T(128)S(1)} %get-tuple-element.3, f32[16]{0:T(128)S(1)} %get-tuple-element.2), channel_id=1, replica_groups=mesh['grid'=8,'band'=4] {'grid'}, use_global_device_ids=true, to_apply=%region_1.0 | all-reduce | flops 32 | bytes 256 | tf_op jit(solution)/shard_map/psum | solution.py:110
  156.1 1.4 multiply_reduce_fusion.1
  157.6 11.8 %psum.45 = f32[16]{0:T(128)S(1)} all-reduce(f32[16]{0:T(128)S(1)} %multiply_reduce_fusion.1), channel_id=1, replica_groups=mesh['grid'=8,'band'=4] {'grid'}, use_global_device_ids=true, to_apply=%region_7.8 | all-reduce | flops 16 | bytes 128 | tf_op jit(solution)/shard_map/psum | solution.py:140
  169.4 1.2 fusion.89
  170.8 3.8 %collective-permute-start.8 = (bf16[16,12288]{1,0:T(8,128)(2,1)S(1)}, bf16[16,12288]{1,0:T(8,128)(2,1)S(1)}, u32[]{:S(2)}, u32[]{:S(2)}) collective-permute-start(bf16[16,12288]{1,0:T(8,128)(2,1)S(1)} %bitcast.56), channel_id=1, source_target_pairs={{0,3},{1,0},{2,1},{3,2},{4,7},{5,4},{6,5},{7,6},{8,11},{9,8},{10,9... | collective-permute-start | bytes 1179656 | tf_op jit(solution)/shard_map/ppermute | solution.py:40
  174.8 9.7 %collective-permute-done.7 = bf16[16,12288]{1,0:T(8,128)(2,1)S(1)} collective-permute-done((bf16[16,12288]{1,0:T(8,128)(2,1)S(1)}, bf16[16,12288]{1,0:T(8,128)(2,1)S(1)}, u32[]{:S(2)}, u32[]{:S(2)}) %collective-permute-start.7) | collective-permute-done | bytes 393248 | tf_op jit(solution)/shard_map/ppermute | solution.py:30
  184.5 4.7 %collective-permute-start.9 = (bf16[16,12288]{1,0:T(8,128)(2,1)S(1)}, bf16[16,12288]{1,0:T(8,128)(2,1)S(1)}, u32[]{:S(2)}, u32[]{:S(2)}) collective-permute-start(bf16[16,12288]{1,0:T(8,128)(2,1)S(1)} %collective-permute-done.7), channel_id=1, source_target_pairs={{0,1},{1,2},{2,3},{3,0},{4,5},{5,6},{6,7},{7,4},{8,9},{9,10},{10,1... | collective-permute-start | bytes 1179656 | tf_op jit(solution)/shard_map/ppermute | solution.py:30
  190.2 10.1 %collective-permute-done.9 = bf16[16,12288]{1,0:T(8,128)(2,1)S(1)} collective-permute-done((bf16[16,12288]{1,0:T(8,128)(2,1)S(1)}, bf16[16,12288]{1,0:T(8,128)(2,1)S(1)}, u32[]{:S(2)}, u32[]{:S(2)}) %collective-permute-start.9) | collective-permute-done | bytes 393248 | tf_op jit(solution)/shard_map/ppermute | solution.py:30
  200.4 5.6 %fusion.13 = f32[256,64]{0,1:T(8,128)} fusion(bf16[64,12288]{1,0:T(8,128)(2,1)S(1)} %constant_dynamic-update-slice_fusion, bf16[32,8,96,128]{3,2,1,0:T(8,128)(2,1)} %bitcast.45), kind=kOutput, calls=%fused_computation.49 | convolution fusion | flops 402653184 | bytes 7929856 | tf_op jit(solution)/shard_map/dot_general | solution.py:118
  206.3 48.7 %all-reduce.8.cloned.1.call-done = f32[256,64]{0,1:T(8,128)} async-done(((f32[256,64]{0,1:T(8,128)}), f32[256,64]{0,1:T(8,128)}) %all-reduce.8.cloned.1.call-update) | async-done | bytes 65552 | tf_op jit(solution)/shard_map/psum | solution.py:124
  254.9 6.1 %convolution_convert_fusion = bf16[64,12288]{1,0:T(8,128)(2,1)} fusion(bf16[32,8,96,128]{3,2,1,0:T(8,128)(2,1)} %bitcast.46, f32[256,64]{0,1:T(8,128)} %all-reduce.8.cloned.1.call-done), kind=kOutput, calls=%fused_computation.32 | convolution fusion | flops 403472384 | bytes 7929856 | tf_op jit(solution)/shard_map/dot_general | solution.py:127
  261.1 1.3 collective-permute-start.6
  262.4 3.1 collective-permute-start.5
  265.5 1.3 collective-permute-done.5
  267.0 29.0 %reduce-scatter.5.cloned.1.call-done = bf16[16,12288]{1,0:T(8,128)(2,1)} async-done(((bf16[64,12288]{1,0:T(8,128)(2,1)}), bf16[16,12288]{1,0:T(8,128)(2,1)}) %reduce-scatter.5.cloned.1.call-update) | async-done | bytes 393232 | tf_op jit(solution)/shard_map/reduce_scatter | solution.py:126
  297.2 3.1 multiply_reduce_fusion
  300.3 13.4 %psum.47 = f32[16]{0:T(128)S(1)} all-reduce(f32[16]{0:T(128)S(1)} %get-tuple-element.6), channel_id=1, replica_groups=mesh['grid'=8,'band'=4] {'grid'}, use_global_device_ids=true, to_apply=%region_11.12 | all-reduce | flops 16 | bytes 128 | tf_op jit(solution)/shard_map/psum | solution.py:135
  313.8 3.2 multiply_subtract_fusion
  (46 shorter events, 5.2 us)
Async XLA Ops:
  7.2 90.1 %all-reduce.6.cloned.1.call-start = ((), (), s32[]{:S(2)}) async-start(), calls=%async_computation.2 | async-start | bytes 131072 | tf_op jit(solution)/shard_map/psum | solution.py:124
  8.6 15.1 %collective-permute-start.2 = (bf16[16,12288]{1,0:T(8,128)(2,1)S(1)}, bf16[16,12288]{1,0:T(8,128)(2,1)S(1)}, u32[]{:S(2)}, u32[]{:S(2)}) collective-permute-start(bf16[16,12288]{1,0:T(8,128)(2,1)S(1)} %bitcast.53), channel_id=1, source_target_pairs={{0,1},{1,2},{2,3},{3,0},{4,5},{5,6},{6,7},{7,4},{8,9},{9,10},{10,1... | collective-permute-start | bytes 1179656 | tf_op jit(solution)/shard_map/ppermute | solution.py:30
  11.6 19.2 %collective-permute-start.3 = (bf16[16,12288]{1,0:T(8,128)(2,1)S(1)}, bf16[16,12288]{1,0:T(8,128)(2,1)S(1)}, u32[]{:S(2)}, u32[]{:S(2)}) collective-permute-start(bf16[16,12288]{1,0:T(8,128)(2,1)S(1)} %bitcast.54), channel_id=1, source_target_pairs={{0,3},{1,0},{2,1},{3,2},{4,7},{5,4},{6,5},{7,6},{8,11},{9,8},{10,9... | collective-permute-start | bytes 1179656 | tf_op jit(solution)/shard_map/ppermute | solution.py:40
  23.7 16.0 %collective-permute-start.4 = (bf16[16,12288]{1,0:T(8,128)(2,1)S(1)}, bf16[16,12288]{1,0:T(8,128)(2,1)S(1)}, u32[]{:S(2)}, u32[]{:S(2)}) collective-permute-start(bf16[16,12288]{1,0:T(8,128)(2,1)S(1)} %collective-permute-done.2), channel_id=1, source_target_pairs={{0,1},{1,2},{2,3},{3,0},{4,5},{5,6},{6,7},{7,4},{8,9},{9,10},{10,1... | collective-permute-start | bytes 1179656 | tf_op jit(solution)/shard_map/ppermute | solution.py:30
  45.3 93.0 %reduce-scatter.3.cloned.1.call-start = ((), (), s32[]{:S(2)}) async-start(), calls=%async_computation.3 | async-start | bytes 1966080 | tf_op jit(solution)/shard_map/reduce_scatter | solution.py:126
  103.4 151.5 %all-reduce.8.cloned.1.call-start = ((), (), s32[]{:S(2)}) async-start(), calls=%async_computation.4 | async-start | bytes 131072 | tf_op jit(solution)/shard_map/psum | solution.py:124
  103.5 4.4 %collective-permute-start.1 = (bf16[16,4,24,128]{3,2,1,0:T(8,128)(2,1)S(1)}, bf16[16,4,24,128]{3,2,1,0:T(8,128)(2,1)S(1)}, u32[]{:S(2)}, u32[]{:S(2)}) collective-permute-start(bf16[16,4,24,128]{3,2,1,0:T(8,128)(2,1)S(1)} %convert_element_type.31), channel_id=1, source_target_pairs={{4,0},{8,4},{12,8},{16,12},{20,16},{24,20},{28,24},{5,1},{9,5},{13... | collective-permute-start | bytes 1179656 | tf_op jit(solution)/shard_map/ppermute | solution.py:59
  104.8 4.4 %collective-permute-start = (bf16[16,4,24,128]{3,2,1,0:T(8,128)(2,1)S(1)}, bf16[16,4,24,128]{3,2,1,0:T(8,128)(2,1)S(1)}, u32[]{:S(2)}, u32[]{:S(2)}) collective-permute-start(bf16[16,4,24,128]{3,2,1,0:T(8,128)(2,1)S(1)} %convert_element_type.31), channel_id=1, source_target_pairs={{0,4},{4,8},{8,12},{12,16},{16,20},{20,24},{24,28},{1,5},{5,9},{9,... | collective-permute-start | bytes 1179656 | tf_op jit(solution)/shard_map/ppermute | solution.py:58
  109.3 30.2 %copy-start = (f32[16,4,24,128]{3,2,1,0:T(8,128)S(1)}, f32[16,4,24,128]{3,2,1,0:T(8,128)}, u32[]{:S(2)}) copy-start(f32[16,4,24,128]{3,2,1,0:T(8,128)} %param.7) | copy-start | bytes 2359300
  109.3 30.2 %copy-start.3 = (f32[4,24,128]{2,1,0:T(8,128)S(1)}, f32[4,24,128]{2,1,0:T(8,128)}, u32[]{:S(2)}) copy-start(f32[4,24,128]{2,1,0:T(8,128)} %param.5) | copy-start | bytes 147460
  109.4 30.2 %copy-start.5 = (f32[16]{0:T(128)S(1)}, f32[16]{0:T(128)}, u32[]{:S(2)}) copy-start(f32[16]{0:T(128)} %param.6) | copy-start | bytes 196
  142.6 26.8 %copy-start.1 = (f32[16,4,24,128]{3,2,1,0:T(8,128)S(1)}, f32[16,4,24,128]{3,2,1,0:T(8,128)}, u32[]{:S(2)}) copy-start(f32[16,4,24,128]{3,2,1,0:T(8,128)} %get-tuple-element.10) | copy-start | bytes 2359300
  170.7 13.8 %collective-permute-start.7 = (bf16[16,12288]{1,0:T(8,128)(2,1)S(1)}, bf16[16,12288]{1,0:T(8,128)(2,1)S(1)}, u32[]{:S(2)}, u32[]{:S(2)}) collective-permute-start(bf16[16,12288]{1,0:T(8,128)(2,1)S(1)} %bitcast.55), channel_id=1, source_target_pairs={{0,1},{1,2},{2,3},{3,0},{4,5},{5,6},{6,7},{7,4},{8,9},{9,10},{10,1... | collective-permute-start | bytes 1179656 | tf_op jit(solution)/shard_map/ppermute | solution.py:30
  170.8 19.4 %collective-permute-start.8 = (bf16[16,12288]{1,0:T(8,128)(2,1)S(1)}, bf16[16,12288]{1,0:T(8,128)(2,1)S(1)}, u32[]{:S(2)}, u32[]{:S(2)}) collective-permute-start(bf16[16,12288]{1,0:T(8,128)(2,1)S(1)} %bitcast.56), channel_id=1, source_target_pairs={{0,3},{1,0},{2,1},{3,2},{4,7},{5,4},{6,5},{7,6},{8,11},{9,8},{10,9... | collective-permute-start | bytes 1179656 | tf_op jit(solution)/shard_map/ppermute | solution.py:40
  184.5 15.8 %collective-permute-start.9 = (bf16[16,12288]{1,0:T(8,128)(2,1)S(1)}, bf16[16,12288]{1,0:T(8,128)(2,1)S(1)}, u32[]{:S(2)}, u32[]{:S(2)}) collective-permute-start(bf16[16,12288]{1,0:T(8,128)(2,1)S(1)} %collective-permute-done.7), channel_id=1, source_target_pairs={{0,1},{1,2},{2,3},{3,0},{4,5},{5,6},{6,7},{7,4},{8,9},{9,10},{10,1... | collective-permute-start | bytes 1179656 | tf_op jit(solution)/shard_map/ppermute | solution.py:30
  206.0 89.9 %reduce-scatter.5.cloned.1.call-start = ((), (), s32[]{:S(2)}) async-start(), calls=%async_computation.5 | async-start | bytes 1966080 | tf_op jit(solution)/shard_map/reduce_scatter | solution.py:126
  261.1 4.4 %collective-permute-start.6 = (bf16[16,4,24,128]{3,2,1,0:T(8,128)(2,1)S(1)}, bf16[16,4,24,128]{3,2,1,0:T(8,128)(2,1)S(1)}, u32[]{:S(2)}, u32[]{:S(2)}) collective-permute-start(bf16[16,4,24,128]{3,2,1,0:T(8,128)(2,1)S(1)} %get-tuple-element.8), channel_id=1, source_target_pairs={{4,0},{8,4},{12,8},{16,12},{20,16},{24,20},{28,24},{5,1},{9,5},{13... | collective-permute-start | bytes 1179656 | tf_op jit(solution)/shard_map/ppermute | solution.py:59
  262.4 4.4 %collective-permute-start.5 = (bf16[16,4,24,128]{3,2,1,0:T(8,128)(2,1)S(1)}, bf16[16,4,24,128]{3,2,1,0:T(8,128)(2,1)S(1)}, u32[]{:S(2)}, u32[]{:S(2)}) collective-permute-start(bf16[16,4,24,128]{3,2,1,0:T(8,128)(2,1)S(1)} %get-tuple-element.8), channel_id=1, source_target_pairs={{0,4},{4,8},{8,12},{12,16},{16,20},{20,24},{24,28},{1,5},{5,9},{9,... | collective-permute-start | bytes 1179656 | tf_op jit(solution)/shard_map/ppermute | solution.py:58
  267.0 30.3 %copy-start.4 = (f32[4,24,128]{2,1,0:T(8,128)S(1)}, f32[4,24,128]{2,1,0:T(8,128)}, u32[]{:S(2)}) copy-start(f32[4,24,128]{2,1,0:T(8,128)} %param.5) | copy-start | bytes 147460
  295.9 1.3 copy-start.2
Sparse Core Ops, SparseCore 0:
  45.4 51.7 all-reduce.5
  103.6 34.6 reduce-scatter.2
  206.1 48.7 all-reduce.7
  261.2 34.6 reduce-scatter.4
